TPU v7x, 256 devices: a whole 4x4x8 slice. The times are simulated.
256 devices in a mesh: segment: 4 (over x), dp: 64 (over y, z, core).
Axes of the slice: x: 4, y: 4, z: 8, core: 2. Of those that a mesh axis runs over, the one named last changes fastest.
Arguments:
- tokens: bfloat16 [32768, 8192], P('dp', 'segment'), may hold values from -16 to 16
- block_values: bfloat16 [8192, 768], P('segment'), may hold values from -0.09375 to 0.09375
- column_blocks: int32 [128, 12], P('segment'), may hold values from 0 to 15, as said below
- counts: int32 [128], P('segment'), may hold values from 4 to 12, as said below
- cotangent: bfloat16 [32768, 1024], P(('dp', 'segment')), may hold values from -6 to 6
Outputs:
- activation: bfloat16 [32768, 1024], P(('dp', 'segment'))
- input_grad: bfloat16 [32768, 8192], P('dp', 'segment')
- weight_grad: float32 [8192, 768], P(('segment', 'dp'))
Inputs may be any that keep to these rules, and one draw needn't show every extreme that they name: `column_blocks`: the first counts[r] entries of row r are distinct column blocks; entries at later slots are column blocks too and are ignored. `counts`: some row block uses all 12 slots.
All inputs are finite; a program needn't handle non-finite values.
Results may differ from a plain program's by a relative error of at most 0.001.
Values may be sent and summed in bfloat16 or wider, within the bound.
No kernel may reach another device: no remote copies, remote signals or barrier semaphores. Data moves between devices by JAX's collectives and lax.ppermute only.
A program may use at most 128 MiB of HBM per device.

v0:
```python
import jax
import jax.numpy as jnp
from jax import lax
from jax.sharding import PartitionSpec as P


def block_onehot(column_blocks, counts, col_blocks):
    slots = column_blocks.shape[1]
    named = column_blocks[:, :, None] == jnp.arange(col_blocks, dtype=jnp.int32)[None, None, :]
    alive = jnp.arange(slots, dtype=jnp.int32)[None, :, None] < counts[:, None, None]
    return named & alive


def select_slots(dense_rows, first_row, column_blocks, counts, block, col_blocks):
    row_count = dense_rows.shape[0]
    slots = column_blocks.shape[1]
    row_block = (first_row + jnp.arange(row_count, dtype=jnp.int32)) // block
    block_ids = jnp.take(column_blocks, row_block, axis=0)
    live_count = jnp.take(counts, row_block, axis=0)
    onehot = block_onehot(block_ids, live_count, col_blocks).astype(jnp.float32)
    picked = jnp.einsum(
        "rkc,rcj->rkj",
        onehot,
        dense_rows.reshape(row_count, col_blocks, block),
        precision=lax.Precision.HIGHEST,
    )
    return picked.reshape(row_count, slots * block)


def per_device(tokens, block_values, column_blocks, counts, cotangent):
    local_rows, features = tokens.shape
    width = cotangent.shape[1]
    row_blocks, slots = column_blocks.shape
    block = features // row_blocks
    col_blocks = width // block
    sections = lax.axis_size("segment")
    replicas = lax.axis_size("dp")
    onehot = block_onehot(column_blocks, counts, col_blocks).astype(jnp.bfloat16)
    blocks_view = block_values.reshape(row_blocks, block, slots, block)
    weight = (
        jnp.einsum("bkc,bikj->bicj", onehot, blocks_view, preferred_element_type=jnp.float32)
        .astype(jnp.bfloat16)
        .reshape(features, width)
    )
    share_rows = local_rows // sections
    own_start = lax.axis_index("segment") * share_rows
    partial_value = jnp.dot(tokens, weight, preferred_element_type=jnp.float32)
    preact_all = lax.psum(partial_value, "segment")
    cotangent_all = lax.all_gather(cotangent, "segment", axis=0, tiled=True)
    activation = lax.dynamic_slice_in_dim(preact_all, own_start, share_rows, 0).astype(jnp.bfloat16)
    owned_rows = features // replicas
    product = lax.dot_general(
        tokens, cotangent_all, (((0,), (0,)), ((), ())), preferred_element_type=jnp.float32
    )
    summed = lax.psum_scatter(product / replicas, "dp", scatter_dimension=0, tiled=True)
    weight_grad = select_slots(
        summed, lax.axis_index("dp") * owned_rows, column_blocks, counts, block, col_blocks
    )
    input_grad = lax.dot_general(
        cotangent_all, weight, (((1,), (1,)), ((), ())), preferred_element_type=jnp.float32
    ).astype(jnp.bfloat16)
    return (activation, input_grad, weight_grad)


def solution(mesh):
    in_specs = (
        P("dp", "segment"),
        P("segment", None),
        P("segment", None),
        P("segment"),
        P(("dp", "segment"), None),
    )
    out_specs = (P(("dp", "segment"), None), P("dp", "segment"), P(("segment", "dp"), None))
    return jax.shard_map(
        per_device, mesh=mesh, in_specs=in_specs, out_specs=out_specs, check_vma=False
    )
```

profile of v0, /device:TPU:2, one launch (start us, length us, event | category | flops | bytes accessed | tf_op | source)
XLA Modules:
  0.0 208.3 jit_solution(9606807791745923992)
XLA Ops:
  7.2 0.0 all-gather.2.cloned.1.call-start
  7.2 0.7 all-gather.2.cloned.1.call-update
  7.9 0.0 reduce-scatter.2.cloned.1.call-start
  8.0 30.3 %all-gather.2.cloned.1.call-done = bf16[512,1024]{1,0:T(8,128)(2,1)} async-done(((bf16[128,1024]{1,0:T(8,128)(2,1)}), bf16[512,1024]{1,0:T(8,128)(2,1)}) %all-gather.2.cloned.1.call-update) | async-done | bytes 1048592 | tf_op jit(solution)/shard_map/all_gather | solution.py:49
  38.3 6.8 %convolution_multiply_fusion = f32[2048,1024]{1,0:T(8,128)} fusion(bf16[512,2048]{1,0:T(8,128)(2,1)S(1)} %copy-done, bf16[512,1024]{1,0:T(8,128)(2,1)} %all-gather.2.cloned.1.call-done), kind=kOutput, calls=%fused_computation.3 | convolution fusion | flops 2149580800 | bytes 11534336 | tf_op jit(solution)/shard_map/dot_general | solution.py:52
  45.1 0.0 reduce-scatter.2.cloned.1.call-update
  45.1 10.6 %reshape.199 = bf16[32,64,12,64]{3,2,1,0:T(8,128)(2,1)} reshape(bf16[2048,768]{1,0:T(8,128)(2,1)} %param.6) | data formatting | bytes 6291456 | tf_op jit(solution)/shard_map/reshape | solution.py:39
  55.7 0.1 copy.12
  55.9 0.6 gather_fusion
  56.4 0.7 gather_fusion.1
  57.1 0.1 iota_compare_fusion.3
  57.2 9.1 %convert_bitcast_fusion = bf16[32,64,16,64]{3,2,1,0:T(8,128)(2,1)} fusion(bf16[32,64,12,64]{3,2,1,0:T(8,128)(2,1)} %reshape.199, s32[32,12]{1,0:T(8,128)S(1)} %copy.12, pred[32,12]{1,0:T(8,128)(4,1)S(1)} %iota_compare_fusion.3), kind=kOutput, calls=%fused_computation.2 | convolution fusion | flops 52441088 | bytes 7341952 | tf_op jit(solution)/shard_map/bkc,bikj->bicj/dot_general | solution.py:41
  66.3 12.0 %reshape.179 = bf16[2048,1024]{1,0:T(8,128)(2,1)} reshape(bf16[32,64,16,64]{3,2,1,0:T(8,128)(2,1)} %convert_bitcast_fusion) | data formatting | bytes 8388608 | tf_op jit(solution)/shard_map/reshape | solution.py:43
  78.3 6.0 %convolution_bitcast_fusion = f32[512,1024]{0,1:T(8,128)} fusion(bf16[2048,1024]{1,0:T(8,128)(2,1)} %reshape.179, bf16[512,2048]{1,0:T(8,128)(2,1)S(1)} %copy-done), kind=kOutput, calls=%fused_computation.6 | convolution fusion | flops 2147483648 | bytes 8388608 | tf_op jit(solution)/shard_map/dot_general | solution.py:47
  84.3 41.4 %all-reduce.1 = bf16[512,1024]{0,1:T(8,128)(2,1)S(1)} all-reduce(f32[512,1024]{0,1:T(8,128)} %convolution_bitcast_fusion), channel_id=1, replica_groups=mesh['segment'=4,'dp'=64] {'segment'}, use_global_device_ids=true, to_apply=%region_0.0 | all-reduce | flops 524288 | bytes 3145728 | tf_op jit(solution)/shard_map/psum | solution.py:48
  125.8 0.9 copy.16
  126.7 0.1 iota_compare_fusion.2
  126.8 0.1 broadcast_select_fusion
  126.9 6.2 %fusion = bf16[512,2048]{0,1:T(8,128)(2,1)} fusion(bf16[2048,1024]{1,0:T(8,128)(2,1)} %reshape.179, bf16[512,1024]{1,0:T(8,128)(2,1)} %all-gather.2.cloned.1.call-done), kind=kOutput, calls=%fused_computation.5 | convolution fusion | flops 2148532224 | bytes 7340032 | tf_op jit(solution)/shard_map/dot_general | solution.py:59
  133.1 3.9 %copy.17 = bf16[512,2048]{1,0:T(8,128)(2,1)} copy(bf16[512,2048]{0,1:T(8,128)(2,1)} %fusion) | data formatting | bytes 4194304
  137.0 62.2 %reduce-scatter.2.cloned.1.call-done = f32[32,1024]{1,0:T(8,128)} async-done(((f32[2048,1024]{1,0:T(8,128)}), f32[32,1024]{1,0:T(8,128)}) %reduce-scatter.2.cloned.1.call-update) | async-done | bytes 131088 | tf_op jit(solution)/shard_map/reduce_scatter | solution.py:55
  199.3 1.0 reshape.180
  200.3 0.4 fusion.5
  200.7 0.7 reshape.181
  (11 shorter events, 0.1 us)
Async XLA Ops:
  7.2 31.1 %copy-start = (bf16[512,2048]{1,0:T(8,128)(2,1)S(1)}, bf16[512,2048]{1,0:T(8,128)(2,1)}, u32[]{:S(2)}) copy-start(bf16[512,2048]{1,0:T(8,128)(2,1)} %param.5) | copy-start | bytes 6291460
  7.2 31.1 %all-gather.2.cloned.1.call-start = ((), (), s32[]{:S(2)}) async-start(), calls=%async_computation.1 | async-start | bytes 1310720 | tf_op jit(solution)/shard_map/all_gather | solution.py:49
  7.9 191.3 %reduce-scatter.2.cloned.1.call-start = ((), (), s32[]{:S(2)}) async-start(), calls=%async_computation.2 | async-start | bytes 8519680 | tf_op jit(solution)/shard_map/reduce_scatter | solution.py:55
  45.1 10.6 %copy-start.2 = (s32[32,12]{0,1:T(8,128)S(1)}, s32[32,12]{0,1:T(8,128)}, u32[]{:S(2)}) copy-start(s32[32,12]{0,1:T(8,128)} %param.7) | copy-start | bytes 4612
  45.1 11.3 %copy-start.1 = (s32[32]{0:T(128)S(1)}, s32[32]{0:T(128)}, u32[]{:S(2)}) copy-start(s32[32]{0:T(128)} %param.8) | copy-start | bytes 388
Sparse Core Ops, SparseCore 0:
  9.8 28.4 all-gather.1
  45.2 153.9 reduce-scatter.1
where the time goes:
time: 209 us; the launch traced here: 208 us
  waiting for transfers between devices  93.2 us (45%)
  blocking collectives  41.4 us (20%)
  local copies, waits for them, and re-layouts  30.6 us (15%)
  matrix products  28.6 us (14%)
  between operations  14.1 us (7%)
    reduce_scatter x1, waiting for transfers between devices, per_device(): lax.psum_scatter(product / replicas, 'dp', scatter_dimension=0, tiled=True)  62.2 us
    psum x1, blocking collectives, per_device(): preact_all = lax.psum(partial_value, 'segment')  41.4 us
    all_gather x1, waiting for transfers between devices, per_device(): cotangent_all = lax.all_gather(cotangent, 'segment', axis=0, tiled=True)  30.3 us
    reshape x1, local copies, waits for them, and re-layouts, per_device(): weight = jnp.einsum('bkc,bikj->bicj', onehot, blocks_view, preferred_elem...  12 us
    reshape x1, local copies, waits for them, and re-layouts, per_device(): blocks_view = block_values.reshape(row_blocks, block, slots, block)  10.6 us
    dot_general x1, matrix products, per_device(): jnp.einsum('bkc,bikj->bicj', onehot, blocks_view, preferred_element_type=...  9.11 us
    dot_general x1, matrix products, per_device(): lax.dot_general(tokens, cotangent_all, (((0,), (0,)), ((), ())), preferre...  6.82 us
    dot_general x1, matrix products, per_device(): lax.dot_general(cotangent_all, weight, (((1,), (1,)), ((), ())), preferre...  6.23 us
  transfers between devices with their start and end apart: 2, of which 2 were waited for; matrix products, arithmetic and copies ran while one was open for 24% of the time, Pallas kernels for 0%

commit v1 on v0

--- a/solution.py
+++ b/solution.py
@@ -1,7 +1,23 @@
+import functools
 import jax
 import jax.numpy as jnp
 from jax import lax
 from jax.sharding import PartitionSpec as P
+
+
+def tell_target_on(unit, row_axis):
+    return jnp.concatenate(
+        jax.lax.all_to_all(
+            jnp.stack(jax.lax.psum(1, axis_name=row_axis) * [unit], 0),
+            axis_name=row_axis,
+            split_axis=0,
+            concat_axis=0,
+        ),
+        0,
+    )
+
+
+recover_goods = functools.partial(tell_target_on, row_axis="segment")
 
 
 def block_onehot(column_blocks, counts, col_blocks):
@@ -46,7 +62,7 @@
     own_start = lax.axis_index("segment") * share_rows
     partial_value = jnp.dot(tokens, weight, preferred_element_type=jnp.float32)
     preact_all = lax.psum(partial_value, "segment")
-    cotangent_all = lax.all_gather(cotangent, "segment", axis=0, tiled=True)
+    cotangent_all = recover_goods(cotangent)
     activation = lax.dynamic_slice_in_dim(preact_all, own_start, share_rows, 0).astype(jnp.bfloat16)
     owned_rows = features // replicas
     product = lax.dot_general(

time: 209 us -> 198 us (0.947)
  waiting for transfers between devices: 93.2 us -> 62.5 us
  blocking collectives: 41.4 us -> 59.9 us
  local copies, waits for them, and re-layouts: 30.6 us -> 32.8 us
    all_gather x1 -> x0, waiting for transfers between devices: 30.3 us -> none  [per_device(): cotangent_all = lax.all_gather(cotangent, 'segment', axis=0, tiled=True)]
    all_to_all x0 -> x1, blocking collectives: none -> 18.3 us  [tell_target_on(): jax.lax.all_to_all(jnp.stack(jax.lax.psum(1, axis_name=row_axis) * [unit]...]
    unnamed x9 -> x11, local copies, waits for them, and re-layouts: 4.89 us -> 5.94 us
  transfers between devices with their start and end apart: 2 -> 1, of which waited for: 2 -> 1; matrix products, arithmetic and copies ran while one was open for 24% -> 26% of each run, Pallas kernels for 0% -> 0%
where the time goes in v1:
time: 198 us; the launch traced here: 197 us
  waiting for transfers between devices  62.5 us (32%)
  blocking collectives  59.9 us (30%)
  local copies, waits for them, and re-layouts  32.8 us (17%)
  matrix products  27.4 us (14%)
  between operations  14.1 us (7%)
    reduce_scatter x1, waiting for transfers between devices, per_device(): lax.psum_scatter(product / replicas, 'dp', scatter_dimension=0, tiled=True)  62.4 us
    psum x1, blocking collectives, per_device(): preact_all = lax.psum(partial_value, 'segment')  41.6 us
    all_to_all x1, blocking collectives, tell_target_on(): jax.lax.all_to_all(jnp.stack(jax.lax.psum(1, axis_name=row_axis) * [unit]...  18.3 us
    reshape x1, local copies, waits for them, and re-layouts, per_device(): weight = jnp.einsum('bkc,bikj->bicj', onehot, blocks_view, preferred_elem...  12 us
    reshape x1, local copies, waits for them, and re-layouts, per_device(): blocks_view = block_values.reshape(row_blocks, block, slots, block)  10.6 us
    dot_general x1, matrix products, per_device(): jnp.einsum('bkc,bikj->bicj', onehot, blocks_view, preferred_element_type=...  9.14 us
    dot_general x1, matrix products, per_device(): lax.dot_general(cotangent_all, weight, (((1,), (1,)), ((), ())), preferre...  6.25 us
    dot_general x1, matrix products, per_device(): partial_value = jnp.dot(tokens, weight, preferred_element_type=jnp.float32)  6.01 us
  transfers between devices with their start and end apart: 1, of which 1 were waited for; matrix products, arithmetic and copies ran while one was open for 26% of the time, Pallas kernels for 0%

profile of v1, /device:TPU:2, one launch (start us, length us, event | category | flops | bytes accessed | tf_op | source)
XLA Modules:
  0.0 196.9 jit_solution(832957169809104598)
XLA Ops:
  7.2 0.0 reduce-scatter.2.cloned.1.call-start
  7.2 1.2 stack.2
  8.4 18.3 %all_to_all.5 = bf16[4,128,1024]{2,1,0:T(8,128)(2,1)S(1)} all-to-all(bf16[4,128,1024]{2,1,0:T(8,128)(2,1)S(1)} %stack.2), channel_id=1, replica_groups=mesh['segment'=4,'dp'=64] {'segment'}, dimensions={0} | all-to-all | bytes 2097152 | tf_op jit(solution)/shard_map/all_to_all | solution.py:10
  26.7 1.0 copy-done.2
  27.8 5.6 %convolution_multiply_fusion = f32[2048,1024]{1,0:T(8,128)} fusion(bf16[512,2048]{1,0:T(8,128)(2,1)S(1)} %copy-done, bf16[512,1024]{1,0:T(8,128)(2,1)S(1)} %bitcast.24), kind=kOutput, calls=%fused_computation.3 | convolution fusion | flops 2149580800 | bytes 11534336 | tf_op jit(solution)/shard_map/dot_general | solution.py:68
  33.4 0.0 reduce-scatter.2.cloned.1.call-update
  33.4 10.6 %reshape.205 = bf16[32,64,12,64]{3,2,1,0:T(8,128)(2,1)} reshape(bf16[2048,768]{1,0:T(8,128)(2,1)} %param.6) | data formatting | bytes 6291456 | tf_op jit(solution)/shard_map/reshape | solution.py:55
  44.0 0.1 copy.12
  44.1 0.6 gather_fusion
  44.7 0.7 gather_fusion.1
  45.4 0.1 iota_compare_fusion.3
  45.5 9.1 %convert_bitcast_fusion = bf16[32,64,16,64]{3,2,1,0:T(8,128)(2,1)} fusion(bf16[32,64,12,64]{3,2,1,0:T(8,128)(2,1)} %reshape.205, s32[32,12]{1,0:T(8,128)S(1)} %copy.12, pred[32,12]{1,0:T(8,128)(4,1)S(1)} %iota_compare_fusion.3), kind=kOutput, calls=%fused_computation.2 | convolution fusion | flops 52441088 | bytes 7341952 | tf_op jit(solution)/shard_map/bkc,bikj->bicj/dot_general | solution.py:57
  54.6 12.0 %reshape.184 = bf16[2048,1024]{1,0:T(8,128)(2,1)} reshape(bf16[32,64,16,64]{3,2,1,0:T(8,128)(2,1)} %convert_bitcast_fusion) | data formatting | bytes 8388608 | tf_op jit(solution)/shard_map/reshape | solution.py:59
  66.6 6.0 %convolution_bitcast_fusion = f32[512,1024]{0,1:T(8,128)} fusion(bf16[2048,1024]{1,0:T(8,128)(2,1)} %reshape.184, bf16[512,2048]{1,0:T(8,128)(2,1)S(1)} %copy-done), kind=kOutput, calls=%fused_computation.6 | convolution fusion | flops 2147483648 | bytes 8388608 | tf_op jit(solution)/shard_map/dot_general | solution.py:63
  72.6 41.6 %all-reduce.1 = bf16[512,1024]{0,1:T(8,128)(2,1)S(1)} all-reduce(f32[512,1024]{0,1:T(8,128)} %convolution_bitcast_fusion), channel_id=1, replica_groups=mesh['segment'=4,'dp'=64] {'segment'}, use_global_device_ids=true, to_apply=%region_0.0 | all-reduce | flops 524288 | bytes 3145728 | tf_op jit(solution)/shard_map/psum | solution.py:64
  114.3 0.9 copy.16
  115.1 0.1 iota_compare_fusion.2
  115.2 0.1 broadcast_select_fusion
  115.3 6.2 %fusion = bf16[512,2048]{0,1:T(8,128)(2,1)} fusion(bf16[2048,1024]{1,0:T(8,128)(2,1)} %reshape.184, bf16[512,1024]{1,0:T(8,128)(2,1)} %bitcast.25), kind=kOutput, calls=%fused_computation.5 | convolution fusion | flops 2148532224 | bytes 7340032 | tf_op jit(solution)/shard_map/dot_general | solution.py:75
  121.5 3.9 %copy.17 = bf16[512,2048]{1,0:T(8,128)(2,1)} copy(bf16[512,2048]{0,1:T(8,128)(2,1)} %fusion) | data formatting | bytes 4194304
  125.5 62.4 %reduce-scatter.2.cloned.1.call-done = f32[32,1024]{1,0:T(8,128)} async-done(((f32[2048,1024]{1,0:T(8,128)}), f32[32,1024]{1,0:T(8,128)}) %reduce-scatter.2.cloned.1.call-update) | async-done | bytes 131088 | tf_op jit(solution)/shard_map/reduce_scatter | solution.py:71
  187.9 1.0 reshape.186
  188.9 0.4 fusion.5
  189.3 0.7 reshape.187
  (12 shorter events, 0.1 us)
Async XLA Ops:
  7.2 20.6 %copy-start = (bf16[512,2048]{1,0:T(8,128)(2,1)S(1)}, bf16[512,2048]{1,0:T(8,128)(2,1)}, u32[]{:S(2)}) copy-start(bf16[512,2048]{1,0:T(8,128)(2,1)} %param.5) | copy-start | bytes 6291460
  7.2 180.7 %reduce-scatter.2.cloned.1.call-start = ((), (), s32[]{:S(2)}) async-start(), calls=%async_computation.2 | async-start | bytes 8519680 | tf_op jit(solution)/shard_map/reduce_scatter | solution.py:71
  26.7 1.0 copy-start.2
  33.4 10.6 %copy-start.3 = (s32[32,12]{0,1:T(8,128)S(1)}, s32[32,12]{0,1:T(8,128)}, u32[]{:S(2)}) copy-start(s32[32,12]{0,1:T(8,128)} %param.7) | copy-start | bytes 4612
  33.4 11.3 %copy-start.1 = (s32[32]{0:T(128)S(1)}, s32[32]{0:T(128)}, u32[]{:S(2)}) copy-start(s32[32]{0:T(128)} %param.8) | copy-start | bytes 388
Sparse Core Ops, SparseCore 0:
  33.5 154.3 reduce-scatter.1

commit v2 on v0

--- a/solution.py
+++ b/solution.py
@@ -1,7 +1,15 @@
+import functools
 import jax
 import jax.numpy as jnp
 from jax import lax
 from jax.sharding import PartitionSpec as P
+
+
+def refer_threads_on(inner_x, mesh_ax):
+    return jnp.sum(lax.all_gather(inner_x, mesh_ax), 0)
+
+
+make_digits = functools.partial(refer_threads_on, mesh_ax="segment")
 
 
 def block_onehot(column_blocks, counts, col_blocks):
@@ -45,7 +53,7 @@
     share_rows = local_rows // sections
     own_start = lax.axis_index("segment") * share_rows
     partial_value = jnp.dot(tokens, weight, preferred_element_type=jnp.float32)
-    preact_all = lax.psum(partial_value, "segment")
+    preact_all = make_digits(partial_value)
     cotangent_all = lax.all_gather(cotangent, "segment", axis=0, tiled=True)
     activation = lax.dynamic_slice_in_dim(preact_all, own_start, share_rows, 0).astype(jnp.bfloat16)
     owned_rows = features // replicas

time: 209 us -> 302 us (1.44)
  waiting for transfers between devices: 93.2 us -> 208 us
  blocking collectives: 41.4 us -> 0 us
  local copies, waits for them, and re-layouts: 30.6 us -> 42.2 us
  other arithmetic: 0.27 us -> 8.74 us
    reduce_scatter x1, waiting for transfers between devices: 62.2 us -> 137 us  [per_device(): lax.psum_scatter(product / replicas, 'dp', scatter_dimension=0, tiled=True)]
    all_gather x0 -> x1, waiting for transfers between devices: none -> 70.1 us  [refer_threads_on(): return jnp.sum(lax.all_gather(inner_x, mesh_ax), 0)]
    psum x1 -> x0, blocking collectives: 41.4 us -> none  [per_device(): preact_all = lax.psum(partial_value, 'segment')]
    all_gather x1, waiting for transfers between devices: 30.3 us -> 0.02 us  [per_device(): cotangent_all = lax.all_gather(cotangent, 'segment', axis=0, tiled=True)]
    all_gather x0 -> x1, local copies, waits for them, and re-layouts: none -> 10.8 us  [refer_threads_on(): return jnp.sum(lax.all_gather(inner_x, mesh_ax), 0)]
    reduce_sum x0 -> x1, other arithmetic: none -> 8.47 us  [refer_threads_on(): return jnp.sum(lax.all_gather(inner_x, mesh_ax), 0)]
  transfers between devices with their start and end apart: 2 -> 3, of which waited for: 2 -> 2; matrix products, arithmetic and copies ran while one was open for 24% -> 25% of each run, Pallas kernels for 0% -> 0%
where the time goes in v2:
time: 302 us; the launch traced here: 301 us
  waiting for transfers between devices  208 us (69%)
  local copies, waits for them, and re-layouts  42.2 us (14%)
  matrix products  28 us (9%)
  between operations  13.8 us (5%)
  other arithmetic  8.74 us (3%)
    reduce_scatter x1, waiting for transfers between devices, per_device(): lax.psum_scatter(product / replicas, 'dp', scatter_dimension=0, tiled=True)  137 us
    all_gather x1, waiting for transfers between devices, refer_threads_on(): return jnp.sum(lax.all_gather(inner_x, mesh_ax), 0)  70.1 us
    reshape x1, local copies, waits for them, and re-layouts, per_device(): weight = jnp.einsum('bkc,bikj->bicj', onehot, blocks_view, preferred_elem...  11.9 us
    all_gather x1, local copies, waits for them, and re-layouts, refer_threads_on(): return jnp.sum(lax.all_gather(inner_x, mesh_ax), 0)  10.8 us
    reshape x1, local copies, waits for them, and re-layouts, per_device(): blocks_view = block_values.reshape(row_blocks, block, slots, block)  10.6 us
    dot_general x1, matrix products, per_device(): jnp.einsum('bkc,bikj->bicj', onehot, blocks_view, preferred_element_type=...  8.92 us
    reduce_sum x1, other arithmetic, refer_threads_on(): return jnp.sum(lax.all_gather(inner_x, mesh_ax), 0)  8.47 us
    dot_general x1, matrix products, per_device(): lax.dot_general(tokens, cotangent_all, (((0,), (0,)), ((), ())), preferre...  6.83 us
  transfers between devices with their start and end apart: 3, of which 2 were waited for; matrix products, arithmetic and copies ran while one was open for 25% of the time, Pallas kernels for 0%

profile of v2, /device:TPU:2, one launch (start us, length us, event | category | flops | bytes accessed | tf_op | source)
XLA Modules:
  0.0 301.2 jit_solution(3028232382280027868)
XLA Ops:
  7.2 0.7 all-gather.4.cloned.1.call-update
  7.9 0.0 all-gather.6.cloned.1.call-start
  8.0 0.8 copy.16
  8.7 10.6 %reshape.200 = bf16[32,64,12,64]{3,2,1,0:T(8,128)(2,1)} reshape(bf16[2048,768]{1,0:T(8,128)(2,1)} %param.6) | data formatting | bytes 6291456 | tf_op jit(solution)/shard_map/reshape | solution.py:47
  19.4 0.1 iota_compare_fusion.3
  19.4 8.9 %convert_bitcast_fusion = bf16[32,64,16,64]{3,2,1,0:T(8,128)(2,1)} fusion(bf16[32,64,12,64]{3,2,1,0:T(8,128)(2,1)} %reshape.200, s32[32,12]{1,0:T(8,128)S(1)} %copy.16, pred[32,12]{1,0:T(8,128)(4,1)S(1)} %iota_compare_fusion.3), kind=kOutput, calls=%fused_computation.2 | convolution fusion | flops 52441088 | bytes 7341952 | tf_op jit(solution)/shard_map/bkc,bikj->bicj/dot_general | solution.py:49
  28.4 11.9 %reshape.179 = bf16[2048,1024]{1,0:T(8,128)(2,1)} reshape(bf16[32,64,16,64]{3,2,1,0:T(8,128)(2,1)} %convert_bitcast_fusion) | data formatting | bytes 8388608 | tf_op jit(solution)/shard_map/reshape | solution.py:51
  40.2 5.9 %convolution_bitcast_fusion = f32[512,1024]{0,1:T(8,128)} fusion(bf16[2048,1024]{1,0:T(8,128)(2,1)} %reshape.179, bf16[512,2048]{1,0:T(8,128)(2,1)S(1)} %copy-done), kind=kOutput, calls=%fused_computation.6 | convolution fusion | flops 2147483648 | bytes 8388608 | tf_op jit(solution)/shard_map/dot_general | solution.py:55
  46.2 0.2 reduce-scatter.2.cloned.1.call-start
  46.4 6.8 %convolution_multiply_fusion = f32[2048,1024]{1,0:T(8,128)} fusion(bf16[512,2048]{1,0:T(8,128)(2,1)S(1)} %copy-done, bf16[512,1024]{1,0:T(8,128)(2,1)} %all-gather.4.cloned.1.call-done), kind=kOutput, calls=%fused_computation.3 | convolution fusion | flops 2149580800 | bytes 11534336 | tf_op jit(solution)/shard_map/dot_general | solution.py:60
  53.3 0.7 gather_fusion.1
  54.0 0.6 gather_fusion
  54.6 0.1 iota_compare_fusion.2
  54.7 0.1 broadcast_select_fusion
  54.8 5.9 %fusion = bf16[512,2048]{0,1:T(8,128)(2,1)} fusion(bf16[2048,1024]{1,0:T(8,128)(2,1)} %reshape.179, bf16[512,1024]{1,0:T(8,128)(2,1)S(1)} %copy-done.2), kind=kOutput, calls=%fused_computation.5 | convolution fusion | flops 2148532224 | bytes 7340032 | tf_op jit(solution)/shard_map/dot_general | solution.py:67
  60.7 4.1 %copy.21 = bf16[512,2048]{1,0:T(8,128)(2,1)} copy(bf16[512,2048]{0,1:T(8,128)(2,1)} %fusion) | data formatting | bytes 4194304
  64.8 70.1 %all-gather.6.cloned.1.call-done = f32[2048,1024]{0,1:T(8,128)} async-done(((f32[512,1024]{0,1:T(8,128)}), f32[2048,1024]{0,1:T(8,128)}) %all-gather.6.cloned.1.call-update) | async-done | bytes 8388624 | tf_op jit(solution)/shard_map/all_gather | solution.py:9
  134.9 10.8 %reshape.198 = f32[4,512,1024]{1,0,2:T(4,128)} reshape(f32[2048,1024]{0,1:T(8,128)} %all-gather.6.cloned.1.call-done) | data formatting | bytes 16777216 | tf_op jit(solution)/shard_map/all_gather | solution.py:9
  145.7 8.5 %reduce_sum.9 = bf16[512,1024]{0,1:T(8,128)(2,1)S(1)} reduce(f32[4,512,1024]{1,0,2:T(4,128)} %reshape.198, f32[]{:T(128)} %constant.48.clone.1), dimensions={0}, to_apply=%region_0.0 | reduce | flops 1572864 | bytes 9437188 | tf_op jit(solution)/shard_map/reduce_sum | solution.py:9
  154.3 0.9 copy.20
  155.1 137.5 %reduce-scatter.2.cloned.1.call-done = f32[32,1024]{1,0:T(8,128)} async-done(((f32[2048,1024]{1,0:T(8,128)}), f32[32,1024]{1,0:T(8,128)}) %reduce-scatter.2.cloned.1.call-update) | async-done | bytes 131088 | tf_op jit(solution)/shard_map/reduce_scatter | solution.py:63
  292.6 1.0 reshape.180
  293.6 0.4 fusion.5
  294.0 0.7 reshape.181
  (15 shorter events, 0.2 us)
Async XLA Ops:
  7.2 33.1 %copy-start = (bf16[512,2048]{1,0:T(8,128)(2,1)S(1)}, bf16[512,2048]{1,0:T(8,128)(2,1)}, u32[]{:S(2)}) copy-start(bf16[512,2048]{1,0:T(8,128)(2,1)} %param.5) | copy-start | bytes 6291460
  7.2 39.2 %all-gather.4.cloned.1.call-start = ((), (), s32[]{:S(2)}) async-start(), calls=%async_computation.1 | async-start | bytes 1310720 | tf_op jit(solution)/shard_map/all_gather | solution.py:57
  7.9 127.0 %all-gather.6.cloned.1.call-start = ((), (), s32[]{:S(2)}) async-start(), calls=%async_computation.3 | async-start | bytes 10485760 | tf_op jit(solution)/shard_map/all_gather | solution.py:9
  8.7 10.6 %copy-start.1 = (s32[32]{0:T(128)S(1)}, s32[32]{0:T(128)}, u32[]{:S(2)}) copy-start(s32[32]{0:T(128)} %param.8) | copy-start | bytes 388
  46.2 246.4 %reduce-scatter.2.cloned.1.call-start = ((), (), s32[]{:S(2)}) async-start(), calls=%async_computation.2 | async-start | bytes 8519680 | tf_op jit(solution)/shard_map/reduce_scatter | solution.py:63
  53.2 1.5 copy-start.2
Sparse Core Ops, SparseCore 0:
  9.8 28.4 all-gather.3
  46.3 88.5 all-gather.5
  139.1 153.4 reduce-scatter.1
